TPU v7x, 32 devices: a whole 2x2x4 slice. The times are simulated.
32 devices in a mesh: feat: 8 (over y, x, core), tok: 4 (over z).
Axes of the slice: x: 2, y: 2, z: 4, core: 2. Of those that a mesh axis runs over, the one named last changes fastest.
Arguments:
- residual: bfloat16 [256, 4608], P('tok', 'feat'), may hold values from -700 to 700
- enc_weight: bfloat16 [4608, 8192], P(None, ('feat', 'tok')), may hold values from -0.09375 to 0.09375
- enc_bias: float32 [8192], P(('feat', 'tok')), may hold values from -3 to 3
- threshold: float32 [8192], P(('feat', 'tok')), may hold values from 0.25 to 2.5
- probe_weight: bfloat16 [8192, 16], P(('feat', 'tok')), may hold values from -0.375 to 0.375
- probe_bias: float32 [16], replicated, may hold values from -3 to 3
- labels: int32 [256], replicated, may hold values from 0 to 15
Outputs:
- probe_grad: float32 [8192, 16], P(('feat', 'tok'))
- token_loss: float32 [256], P(('feat', 'tok'))
All inputs are finite; a program needn't handle non-finite values.
Results may differ from a plain program's by a relative error of at most 0.0034.
Values may be sent and summed in bfloat16 or wider, within the bound.
No kernel may reach another device: no remote copies, remote signals or barrier semaphores. Data moves between devices by JAX's collectives and lax.ppermute only.
A program may use at most 64 MiB of HBM per device.

v0:
```python
import jax
import jax.numpy as jnp
from jax import lax
from jax.sharding import PartitionSpec as P

epsilon = 1e-06
smooth_width = 0.125


def normalize(values, squares):
    full_width = values.shape[1] * lax.axis_size("feat")
    row_scale = lax.rsqrt(squares / full_width + epsilon)
    return (values * row_scale[:, None]).astype(jnp.bfloat16)


def local(residual, enc_weight, enc_bias, threshold, probe_weight, probe_bias, labels):
    values = residual.astype(jnp.float32)
    squares = lax.psum(jnp.sum(values * values, axis=1), "feat")
    normed = normalize(values, squares)
    all_tokens = lax.all_gather(normed, "tok", axis=0, tiled=True)
    preact = jnp.dot(
        lax.all_gather(all_tokens, "feat", axis=1, tiled=True),
        enc_weight,
        preferred_element_type=jnp.float32,
    )
    encode_preact = preact
    encode_preact = encode_preact + enc_bias
    features = (encode_preact * jax.nn.sigmoid((encode_preact - threshold) / smooth_width)).astype(
        jnp.bfloat16
    )
    partial_value = jnp.dot(features, probe_weight, preferred_element_type=jnp.float32)
    num_tokens = features.shape[0]
    share_rows = num_tokens // lax.axis_size(("feat", "tok"))
    position = lax.axis_index(("feat", "tok"))
    class_ids = jnp.arange(probe_weight.shape[1], dtype=jnp.int32)
    logits = lax.psum(partial_value, ("feat", "tok"))
    softmax_logits = logits
    softmax_logits = softmax_logits + probe_bias
    exps = jnp.exp(softmax_logits)
    totals = jnp.sum(exps, axis=1, keepdims=True)
    onehot = (labels[:, None] == class_ids[None, :]).astype(jnp.float32)
    losses = jnp.log(totals[:, 0]) - jnp.sum(onehot * softmax_logits, axis=1)
    losses, delta = (losses, (exps / totals - onehot).astype(jnp.bfloat16))
    token_loss = lax.dynamic_slice_in_dim(losses, position * share_rows, share_rows, 0)
    gradient = jnp.dot(features.T, delta, preferred_element_type=jnp.float32)
    return (gradient, token_loss)


def solution(mesh):
    in_specs = (
        P("tok", "feat"),
        P(None, ("feat", "tok")),
        P(("feat", "tok")),
        P(("feat", "tok")),
        P(("feat", "tok"), None),
        P(),
        P(),
    )
    out_specs = (P(("feat", "tok"), None), P(("feat", "tok")))
    return jax.shard_map(local, mesh=mesh, in_specs=in_specs, out_specs=out_specs, check_vma=False)
```

profile of v0, /device:TPU:0, one launch (start us, length us, event | category | flops | bytes accessed | tf_op | source)
XLA Modules:
  0.0 118.5 jit_solution(7145613870447156144)
XLA Ops:
  7.2 0.0 copy-start
  7.2 0.0 all-gather.2.cloned.1.call-start
  7.2 1.2 fusion
  8.4 15.2 %psum.14 = f32[64]{0:T(128)S(1)} all-reduce(f32[64]{0:T(128)S(1)} %fusion), channel_id=1, replica_groups=mesh['feat'=8,'tok'=4] {'feat'}, use_global_device_ids=true, to_apply=%region_1.0 | all-reduce | flops 64 | bytes 512 | tf_op jit(solution)/shard_map/psum | solution.py:18
  23.5 1.0 fusion.1
  24.5 14.9 %all_gather.6 = bf16[256,576]{1,0:T(8,128)(2,1)S(1)} all-gather(bf16[64,576]{1,0:T(8,128)(2,1)S(1)} %fusion.1), channel_id=1, replica_groups=mesh['feat'=8,'tok'=4] {'tok'}, dimensions={0}, use_global_device_ids=true | all-gather | bytes 368640 | tf_op jit(solution)/shard_map/all_gather | solution.py:20
  39.4 0.9 copy.10
  40.3 0.0 all-gather.2.cloned.1.call-update
  40.3 0.0 copy-start.1
  40.3 0.0 copy-start.2
  40.4 0.0 copy-start.3
  40.4 27.8 %all-gather.2.cloned.1.call-done = bf16[256,4608]{0,1:T(8,128)(2,1)} async-done(((bf16[256,576]{0,1:T(8,128)(2,1)}), bf16[256,4608]{0,1:T(8,128)(2,1)}) %all-gather.2.cloned.1.call-update) | async-done | bytes 2359312 | tf_op jit(solution)/shard_map/all_gather | solution.py:22
  68.1 0.0 copy-done
  68.1 2.5 %multiply_convert_fusion = bf16[256,256]{1,0:T(8,128)(2,1)S(1)} fusion(bf16[256,4608]{0,1:T(8,128)(2,1)} %all-gather.2.cloned.1.call-done, bf16[4608,256]{1,0:T(8,128)(2,1)S(1)} %copy-done, f32[256]{0:T(256)} %param.10, f32[256]{0:T(256)} %param.9), kind=kOutput, calls=%fused_computation.1 | convolution fusion | flops 604504064 | bytes 4851712 | tf_op jit(solution)/shard_map/dot_general | solution.py:21
  70.7 0.0 copy-done.1
  70.7 0.1 fusion.6
  70.8 39.3 %psum.15 = f32[256,16]{0,1:T(8,128)S(1)} all-reduce(f32[256,16]{0,1:T(8,128)S(1)} %fusion.6), channel_id=1, replica_groups=mesh['feat'=8,'tok'=4] {'feat','tok'}, use_global_device_ids=true, to_apply=%region_2.0 | all-reduce | flops 4096 | bytes 32768 | tf_op jit(solution)/shard_map/psum | solution.py:36
  110.2 0.0 copy-done.2
  110.2 0.0 copy-done.3
  110.2 0.1 select_reduce_fusion
  110.3 0.8 fusion.2
  111.1 0.6 dynamic_slice.3
  (2 shorter events, 0.0 us)
Async XLA Ops:
  7.2 61.0 %copy-start = (bf16[4608,256]{1,0:T(8,128)(2,1)S(1)}, bf16[4608,256]{1,0:T(8,128)(2,1)}, u32[]{:S(2)}) copy-start(bf16[4608,256]{1,0:T(8,128)(2,1)} %param.8) | copy-start | bytes 7077892
  7.2 60.9 %all-gather.2.cloned.1.call-start = ((), (), s32[]{:S(2)}) async-start(), calls=%async_computation | async-start | bytes 2654208 | tf_op jit(solution)/shard_map/all_gather | solution.py:22
  40.3 30.3 %copy-start.1 = (bf16[256,16]{0,1:T(8,128)(2,1)S(1)}, bf16[256,16]{0,1:T(8,128)(2,1)}, u32[]{:S(2)}) copy-start(bf16[256,16]{0,1:T(8,128)(2,1)} %param.11) | copy-start | bytes 24580
  40.3 69.8 %copy-start.2 = (s32[256]{0:T(256)S(1)}, s32[256]{0:T(256)}, u32[]{:S(2)}) copy-start(s32[256]{0:T(256)} %param.13) | copy-start | bytes 3076
  40.4 69.8 %copy-start.3 = (f32[16]{0:T(128)S(1)}, f32[16]{0:T(128)}, u32[]{:S(2)}) copy-start(f32[16]{0:T(128)} %param.12) | copy-start | bytes 196
Sparse Core Ops, SparseCore 0:
  40.5 27.6 all-gather.1
where the time goes:
time: 119 us
  blocking collectives  69.4 us (58%)
  waiting for transfers between devices  27.8 us (23%)
  between operations  14.1 us (12%)
  matrix products  3.49 us (3%)
  other arithmetic  2.24 us (2%)
  local copies, waits for them, and re-layouts  1.5 us (1%)
    psum x1, blocking collectives, local(): logits = lax.psum(partial_value, ('feat', 'tok'))  39.3 us
    all_gather x1, waiting for transfers between devices, local(): lax.all_gather(all_tokens, 'feat', axis=1, tiled=True)  27.8 us
    psum x1, blocking collectives, local(): squares = lax.psum(jnp.sum(values * values, axis=1), 'feat')  15.2 us
    all_gather x1, blocking collectives, local(): all_tokens = lax.all_gather(normed, 'tok', axis=0, tiled=True)  14.9 us
    dot_general x1, matrix products, local(): jnp.dot(lax.all_gather(all_tokens, 'feat', axis=1, tiled=True), enc_weigh...  2.53 us
  transfers between devices with their start and end apart: 1, of which 1 were waited for; matrix products, arithmetic and copies ran while one was open for 0% of the time, Pallas kernels for 0%

commit v1 on v0

--- a/solution.py
+++ b/solution.py
@@ -33,7 +33,8 @@
     share_rows = num_tokens // lax.axis_size(("feat", "tok"))
     position = lax.axis_index(("feat", "tok"))
     class_ids = jnp.arange(probe_weight.shape[1], dtype=jnp.int32)
-    logits = lax.psum(partial_value, ("feat", "tok"))
+    parts = lax.all_gather(partial_value, ("feat", "tok"))
+    logits = jnp.sum(parts, axis=0)
     softmax_logits = logits
     softmax_logits = softmax_logits + probe_bias
     exps = jnp.exp(softmax_logits)

time: 119 us -> 151 us (1.27)
  blocking collectives: 69.4 us -> 102 us
    all_gather x0 -> x1, blocking collectives: none -> 71.6 us  [local(): parts = lax.all_gather(partial_value, ('feat', 'tok'))]
    psum x1 -> x0, blocking collectives: 39.3 us -> none  [local(): logits = lax.psum(partial_value, ('feat', 'tok'))]
where the time goes in v1:
time: 151 us
  blocking collectives  102 us (68%)
  waiting for transfers between devices  27.8 us (18%)
  between operations  14.1 us (9%)
  matrix products  3.48 us (2%)
  other arithmetic  2.29 us (2%)
  local copies, waits for them, and re-layouts  1.66 us (1%)
    all_gather x1, blocking collectives, local(): parts = lax.all_gather(partial_value, ('feat', 'tok'))  71.6 us
    all_gather x1, waiting for transfers between devices, local(): lax.all_gather(all_tokens, 'feat', axis=1, tiled=True)  27.8 us
    psum x1, blocking collectives, local(): squares = lax.psum(jnp.sum(values * values, axis=1), 'feat')  15.2 us
    all_gather x1, blocking collectives, local(): all_tokens = lax.all_gather(normed, 'tok', axis=0, tiled=True)  14.9 us
  transfers between devices with their start and end apart: 1, of which 1 were waited for; matrix products, arithmetic and copies ran while one was open for 0% of the time, Pallas kernels for 0%

profile of v1, /device:TPU:0, one launch (start us, length us, event | category | flops | bytes accessed | tf_op | source)
XLA Modules:
  0.0 151.0 jit_solution(14659095292995916565)
XLA Ops:
  7.2 0.0 copy-start
  7.2 0.0 all-gather.3.cloned.1.call-start
  7.2 1.2 fusion
  8.4 15.2 %psum.7 = f32[64]{0:T(128)S(1)} all-reduce(f32[64]{0:T(128)S(1)} %fusion), channel_id=1, replica_groups=mesh['feat'=8,'tok'=4] {'feat'}, use_global_device_ids=true, to_apply=%region_1.0 | all-reduce | flops 64 | bytes 512 | tf_op jit(solution)/shard_map/psum | solution.py:18
  23.5 1.0 fusion.1
  24.5 14.9 %all_gather.12 = bf16[256,576]{1,0:T(8,128)(2,1)S(1)} all-gather(bf16[64,576]{1,0:T(8,128)(2,1)S(1)} %fusion.1), channel_id=1, replica_groups=mesh['feat'=8,'tok'=4] {'tok'}, dimensions={0}, use_global_device_ids=true | all-gather | bytes 368640 | tf_op jit(solution)/shard_map/all_gather | solution.py:20
  39.4 0.9 copy.10
  40.3 0.0 all-gather.3.cloned.1.call-update
  40.3 0.0 copy-start.1
  40.3 0.0 copy-start.2
  40.4 0.0 copy-start.3
  40.4 27.8 %all-gather.3.cloned.1.call-done = bf16[256,4608]{0,1:T(8,128)(2,1)} async-done(((bf16[256,576]{0,1:T(8,128)(2,1)}), bf16[256,4608]{0,1:T(8,128)(2,1)}) %all-gather.3.cloned.1.call-update) | async-done | bytes 2359312 | tf_op jit(solution)/shard_map/all_gather | solution.py:22
  68.1 0.0 copy-done
  68.1 2.5 %multiply_convert_fusion = bf16[256,256]{1,0:T(8,128)(2,1)S(1)} fusion(bf16[256,4608]{0,1:T(8,128)(2,1)} %all-gather.3.cloned.1.call-done, bf16[4608,256]{1,0:T(8,128)(2,1)S(1)} %copy-done, f32[256]{0:T(256)} %param.10, f32[256]{0:T(256)} %param.9), kind=kOutput, calls=%fused_computation.2 | convolution fusion | flops 604504064 | bytes 4851712 | tf_op jit(solution)/shard_map/dot_general | solution.py:21
  70.7 0.0 copy-done.1
  70.7 0.1 fusion.6
  70.8 71.6 %all-gather = f32[8192,16]{0,1:T(8,128)S(1)} all-gather(f32[256,16]{0,1:T(8,128)S(1)} %fusion.6), channel_id=2, replica_groups=mesh['feat'=8,'tok'=4] {'feat','tok'}, dimensions={0}, use_global_device_ids=true | all-gather | bytes 540672 | tf_op jit(solution)/shard_map/all_gather | solution.py:36
  142.4 0.2 copy.11
  142.6 0.1 bitcast_reduce_fusion
  142.6 0.0 copy-done.2
  142.6 0.0 copy-done.3
  142.6 0.1 select_reduce_fusion
  142.7 0.8 fusion.2
  143.6 0.6 dynamic_slice.3
  (2 shorter events, 0.0 us)
Async XLA Ops:
  7.2 61.0 %copy-start = (bf16[4608,256]{1,0:T(8,128)(2,1)S(1)}, bf16[4608,256]{1,0:T(8,128)(2,1)}, u32[]{:S(2)}) copy-start(bf16[4608,256]{1,0:T(8,128)(2,1)} %param.8) | copy-start | bytes 7077892
  7.2 60.9 %all-gather.3.cloned.1.call-start = ((), (), s32[]{:S(2)}) async-start(), calls=%async_computation | async-start | bytes 2654208 | tf_op jit(solution)/shard_map/all_gather | solution.py:22
  40.3 30.3 %copy-start.1 = (bf16[256,16]{0,1:T(8,128)(2,1)S(1)}, bf16[256,16]{0,1:T(8,128)(2,1)}, u32[]{:S(2)}) copy-start(bf16[256,16]{0,1:T(8,128)(2,1)} %param.11) | copy-start | bytes 24580
  40.3 102.3 %copy-start.2 = (s32[256]{0:T(256)S(1)}, s32[256]{0:T(256)}, u32[]{:S(2)}) copy-start(s32[256]{0:T(256)} %param.13) | copy-start | bytes 3076
  40.4 102.3 %copy-start.3 = (f32[16]{0:T(128)S(1)}, f32[16]{0:T(128)}, u32[]{:S(2)}) copy-start(f32[16]{0:T(128)} %param.12) | copy-start | bytes 196
Sparse Core Ops, SparseCore 0:
  40.5 27.6 all-gather.2
